TPU v7x, 32 devices: a whole 2x2x4 slice. The times are simulated.
32 devices in a mesh: grp: 2 (over y), tm: 4 (over z), height: 4 (over x, core).
Axes of the slice: x: 2, y: 2, z: 4, core: 2. Of those that a mesh axis runs over, the one named last changes fastest.
Arguments:
- latents: bfloat16 [8, 8, 160, 384], P(('grp', 'tm'), 'height'), parts along dimension 0, may hold values from -6 to 6
- gain: float32 [384], replicated, may hold values from 0.1 to 1.9
- bias: float32 [384], replicated, may hold values from -3 to 3
- weight: bfloat16 [10368, 384], replicated, may hold values from -0.0625 to 0.0625
- cotangent: bfloat16 [8, 8, 160, 384], P(('grp', 'tm'), 'height'), parts along dimension 0, may hold values from -6 to 6
Outputs:
- output: bfloat16 [8, 8, 160, 384], P(('grp', 'tm'), 'height'), parts along dimension 0
- latent_grad: bfloat16 [8, 8, 160, 384], P(('grp', 'tm'), 'height'), parts along dimension 0
- weight_grad: float32 [20736, 384], P(('grp', 'tm'), 'height'), parts along dimension 0
There are 2 independent parts, one for each index of `grp`. A program takes and returns all parts, laid end to end along the dimension named above; an argument that names none is the same for every part. Nothing has to cross between parts.
All inputs are finite; a program needn't handle non-finite values.
Results may differ from a plain program's by a relative error of at most 0.0029.
Values may be sent and summed in bfloat16 or wider, within the bound.
No kernel may reach another device: no remote copies, remote signals or barrier semaphores. Data moves between devices by JAX's collectives and lax.ppermute only.
A program may use at most 128 MiB of HBM per device.

v0:
```python
import math
import jax
import jax.numpy as jnp
from jax import lax
from jax.sharding import PartitionSpec as P


def shifted_2(value, axis, by):
    devices = lax.axis_size(axis)
    pairs = [(i, i + by) for i in range(devices) if 0 <= i + by < devices]
    return lax.ppermute(value, axis, pairs)


def padded(cells, sides, width):
    for axis, dim in sides:
        count = lax.axis_size(axis)
        ends = count - 1
        head = lax.slice_in_dim(cells, 0, width, axis=dim)
        tail = lax.slice_in_dim(cells, cells.shape[dim] - width, cells.shape[dim], axis=dim)
        cells = jnp.concatenate(
            [
                lax.ppermute(tail, axis, [(i, (i + 1) % count) for i in range(ends)]),
                cells,
                lax.ppermute(head, axis, [((i + 1) % count, i) for i in range(ends)]),
            ],
            axis=dim,
        )
    return cells


def forward_arrange(cube):
    depth, rows_t, cols_t, inputs, outputs = cube.shape
    return cube.transpose(0, 1, 3, 2, 4).reshape(9, inputs, 3 * outputs)


def backward_arrange(cube):
    depth, rows_t, cols_t, inputs, outputs = cube.shape
    return cube.transpose(0, 1, 4, 2, 3).reshape(9, outputs, 3 * inputs)


def forward_sum(window, arranged, row_total, col_total):
    width = window.shape[-1]
    slots = arranged.shape[-1] // 3
    total = None
    for depth_tap in range(3):
        for row_tap in range(3):
            slab = window[depth_tap, row_tap : row_tap + row_total].reshape(
                row_total * (col_total + 2), width
            )
            product = jnp.dot(
                slab, arranged[3 * depth_tap + row_tap], preferred_element_type=jnp.float32
            )
            total = product if total is None else total + product
    total = total.reshape(row_total, col_total + 2, 3, slots)
    return (
        total[:, 0:col_total, 0] + total[:, 1 : col_total + 1, 1] + total[:, 2 : col_total + 2, 2]
    )


def backward_sum(window, arranged, row_total, col_total):
    width = window.shape[-1]
    slots = arranged.shape[-1] // 3
    total = None
    for depth_tap in range(3):
        for row_tap in range(3):
            slab = window[2 - depth_tap, 2 - row_tap : 2 - row_tap + row_total].reshape(
                row_total * (col_total + 2), width
            )
            product = jnp.dot(
                slab, arranged[3 * depth_tap + row_tap], preferred_element_type=jnp.float32
            )
            total = product if total is None else total + product
    total = total.reshape(row_total, col_total + 2, 3, slots)
    return (
        total[:, 2 : col_total + 2, 0] + total[:, 1 : col_total + 1, 1] + total[:, 0:col_total, 2]
    )


def weight_terms(window, cot_block, row_total, col_total):
    width = window.shape[-1]
    slots = cot_block.shape[-1]
    flat_count = row_total * (col_total + 2)
    shifted = [
        jnp.pad(cot_block, ((0, 0), (col_tap, 2 - col_tap), (0, 0))).reshape(flat_count, slots)
        for col_tap in range(3)
    ]
    pieces = []
    for depth_tap in range(3):
        for row_tap in range(3):
            slab = window[depth_tap, row_tap : row_tap + row_total].reshape(flat_count, width)
            for col_tap in range(3):
                pieces.append(
                    lax.dot_general(
                        slab,
                        shifted[col_tap],
                        (((0,), (0,)), ((), ())),
                        preferred_element_type=jnp.float32,
                    )
                )
    return jnp.concatenate(pieces, axis=0)


def column_share(cotangent):
    return lax.all_to_all(cotangent, "height", split_axis=3, concat_axis=1, tiled=True)


def local(latents, gain, bias, weight, cotangent):
    frame_count, row_count, col_count, channels = latents.shape
    latent_wide = latents.astype(jnp.float32)
    root_mean = jnp.sqrt(jnp.mean(latent_wide * latent_wide, axis=-1, keepdims=True) + 1e-06)
    normed = latent_wide / root_mean * gain
    hidden = jax.nn.silu(normed).astype(jnp.bfloat16)
    height_count = lax.axis_size("height")
    share_width = channels // height_count
    first_column = lax.axis_index("height") * share_width
    total_rows = row_count * height_count
    tap_rows = 27 * channels
    inverse_root = 1.0 / math.sqrt(lax.axis_size("tm") * total_rows * col_count)
    weight_cube = weight.reshape(3, 3, 3, channels, channels)
    shared_cot = cotangent
    prior = shifted_2(hidden, "tm", 1)
    second = shifted_2(hidden, "tm", 2)
    stacked = jnp.concatenate([second, prior, hidden], axis=0)
    gathered = lax.all_gather(stacked, "height", axis=1, tiled=True)
    framed = jnp.pad(gathered, ((0, 0), (1, 1), (1, 1), (0, 0)))
    shared_cot = column_share(cotangent)
    share_cube = lax.dynamic_slice_in_dim(weight_cube, first_column, share_width, 4)
    share_arranged = forward_arrange(share_cube)

    def block_step(block_index, carry):
        conv_total, grad_total = carry
        first_row = block_index * row_count
        window = lax.dynamic_slice_in_dim(framed, first_row, row_count + 2, 1)
        conv_block = forward_sum(window, share_arranged, row_count, col_count)
        conv_total = lax.dynamic_update_slice_in_dim(conv_total, conv_block, first_row, 0)
        cot_block = lax.dynamic_slice_in_dim(shared_cot[0], first_row, row_count, 0)
        grad_total = grad_total + weight_terms(window, cot_block, row_count, col_count)
        return (conv_total, grad_total)

    start_carry = (
        jnp.zeros((total_rows, col_count, share_width), jnp.float32),
        jnp.zeros((tap_rows, share_width), jnp.float32),
    )
    conv_share, share_terms = lax.fori_loop(0, height_count, block_step, start_carry)
    weight_grad = lax.psum_scatter(
        share_terms * inverse_root, "tm", scatter_dimension=0, tiled=True
    )
    conv_out = lax.all_to_all(
        conv_share.reshape(1, total_rows, col_count, share_width),
        "height",
        split_axis=1,
        concat_axis=3,
        tiled=True,
    )
    output = (latent_wide + conv_out + bias).astype(jnp.bfloat16)
    cotangent_edged = padded(cotangent, (("height", 1),), 1)
    next_frame = shifted_2(cotangent_edged, "tm", -1)
    second_next = shifted_2(cotangent_edged, "tm", -2)
    future_block = jnp.pad(
        jnp.concatenate([cotangent_edged, next_frame, second_next], axis=0),
        ((0, 0), (0, 0), (1, 1), (0, 0)),
    )
    hidden_grad = backward_sum(
        future_block, backward_arrange(weight_cube), row_count, col_count
    ).reshape(frame_count, row_count, col_count, channels)
    sigmoid_pre = jax.nn.sigmoid(normed)
    normed_grad = hidden_grad * sigmoid_pre * (1.0 + normed * (1.0 - sigmoid_pre))
    scaled_grad = normed_grad * gain
    unit_latent = latent_wide / root_mean
    inner = jnp.mean(scaled_grad * unit_latent, axis=-1, keepdims=True)
    latent_grad = (
        cotangent.astype(jnp.float32) + (scaled_grad - unit_latent * inner) / root_mean
    ).astype(jnp.bfloat16)
    return (output, latent_grad, weight_grad)


def solution(mesh):
    placed = (
        P(("grp", "tm"), "height", None, None),
        P(),
        P(),
        P(),
        P(("grp", "tm"), "height", None, None),
    )
    return jax.shard_map(
        local,
        mesh=mesh,
        in_specs=placed,
        out_specs=(
            P(("grp", "tm"), "height", None, None),
            P(("grp", "tm"), "height", None, None),
            P(("grp", "tm"), "height"),
        ),
        check_vma=False,
    )
```

profile of v0, /device:TPU:0, one launch (start us, length us, event | category | flops | bytes accessed | tf_op | source)
XLA Modules:
  0.0 332.8 jit_solution(15227370439125368091)
XLA Ops:
  8.2 2.4 collective-permute-start.2
  12.9 3.0 collective-permute-done.3
  19.6 22.5 %collective-permute-done.5 = bf16[1,4,160,384]{3,2,1,0:T(8,128)(2,1)S(1)} collective-permute-done((bf16[1,4,160,384]{3,2,1,0:T(8,128)(2,1)S(1)}, bf16[1,4,160,384]{3,2,1,0:T(8,128)(2,1)S(1)}, u32[]{:S(2)}, u32[]{:S(2)}) %collective-permute-start.5) | collective-permute-done | bytes 491552 | tf_op jit(solution)/shard_map/ppermute | solution.py:11
  43.4 1.9 fusion.26
  45.3 1.8 convolution_add_fusion.15
  47.2 2.0 convolution_add_fusion.14
  49.1 1.8 convolution_add_fusion.13
  55.8 2.1 multiply_reduce_fusion
  58.0 13.0 %collective-permute-start.1 = (bf16[1,2,160,384]{3,2,1,0:T(8,128)(2,1)S(1)}, bf16[1,2,160,384]{3,2,1,0:T(8,128)(2,1)S(1)}, u32[]{:S(2)}, u32[]{:S(2)}) collective-permute-start(bf16[1,2,160,384]{3,2,1,0:T(8,128)(2,1)S(1)} %get-tuple-element.240), channel_id=1, source_target_pairs={{0,4},{4,8},{8,12},{1,5},{5,9},{9,13},{2,6},{6,10},{10,14},{3,7},{... | collective-permute-start | bytes 737288 | tf_op jit(solution)/shard_map/ppermute | solution.py:11
  72.3 5.0 %collective-permute-done.1 = bf16[1,2,160,384]{3,2,1,0:T(8,128)(2,1)S(1)} collective-permute-done((bf16[1,2,160,384]{3,2,1,0:T(8,128)(2,1)S(1)}, bf16[1,2,160,384]{3,2,1,0:T(8,128)(2,1)S(1)}, u32[]{:S(2)}, u32[]{:S(2)}) %collective-permute-start.1) | collective-permute-done | bytes 245792 | tf_op jit(solution)/shard_map/ppermute | solution.py:11
  77.3 5.3 %collective-permute-done = bf16[1,2,160,384]{3,2,1,0:T(8,128)(2,1)S(1)} collective-permute-done((bf16[1,2,160,384]{3,2,1,0:T(8,128)(2,1)S(1)}, bf16[1,2,160,384]{3,2,1,0:T(8,128)(2,1)S(1)}, u32[]{:S(2)}, u32[]{:S(2)}) %collective-permute-start) | collective-permute-done | bytes 245792 | tf_op jit(solution)/shard_map/ppermute | solution.py:11
  84.8 3.5 %all-to-all-start = ((bf16[1,2,160,384]{2,1,0,3:T(2,128)(2,1)}), bf16[1,2,160,384]{2,1,0,3:T(2,128)(2,1)S(1)}, u32[]{:S(2)}, u32[]{:S(2)}) async-start(bf16[1,2,160,384]{2,1,0,3:T(2,128)(2,1)} %copy.31), calls=%async_computation | async-start | bytes 786432 | tf_op jit(solution)/shard_map/all_to_all | solution.py:104
  88.3 3.5 %dynamic-slice_bitcast_fusion.1 = bf16[3,3,384,3,96]{4,2,3,1,0:T(8,128)(2,1)S(1)} fusion(bf16[3,3,3,384,384]{4,3,2,1,0:T(8,128)(2,1)} %bitcast.310, s32[]{:T(128)S(6)} %select_n.24), kind=kLoop, calls=%fused_computation.80 | loop fusion | bytes 3981316 | tf_op jit(solution)/shard_map/transpose | solution.py:33
  91.8 2.6 copy.30
  94.4 4.4 %copy.33 = bf16[9,384,288]{2,1,0:T(8,128)(2,1)} copy(bf16[9,384,288]{1,2,0:T(8,128)(2,1)} %bitcast.318) | data formatting | bytes 3981312
  99.2 16.5 %all-gather.2.cloned.1.call-done = bf16[3,8,160,384]{3,2,1,0:T(8,128)(2,1)} async-done(((bf16[3,2,160,384]{3,2,1,0:T(8,128)(2,1)}), bf16[3,8,160,384]{3,2,1,0:T(8,128)(2,1)}) %all-gather.2.cloned.1.call-update) | async-done | bytes 2949136 | tf_op jit(solution)/shard_map/all_gather | solution.py:124
  115.6 4.9 %pad.41 = bf16[3,10,162,384]{3,2,1,0:T(8,128)(2,1)} pad(bf16[3,8,160,384]{3,2,1,0:T(8,128)(2,1)} %all-gather.2.cloned.1.call-done, bf16[]{:T(256)} %constant.82.clone.1), padding=0_0x1_1x1_1x0_0 | pad | bytes 6681602 | tf_op jit(solution)/shard_map/jit(_pad)/pad | solution.py:125
  121.4 94.6 %while.18 = (s32[]{:T(128)}, f32[8,160,96]{2,1,0:T(8,128)}, f32[10368,96]{0,1:T(8,128)}, bf16[3,10,162,384]{3,2,1,0:T(8,128)(2,1)}, bf16[9,384,288]{2,1,0:T(8,12...) while((s32[]{:T(128)}, f32[8,160,96]{2,1,0:T(8,128)}, ...), condition=%wide.region_2.3_spmd.clone, body=%wide.region_1.2_spmd.clone.sunk | while | flops 1292743680 | bytes 89893304 | solution.py:144
  122.3 2.0 constant_dynamic-slice_fusion.10
  124.8 1.5 fusion.258
  126.3 1.3 convolution_add_fusion.24
  127.7 1.3 convolution_add_fusion.25
  132.1 1.5 reshape.142
  143.2 1.9 copy-done.1
  146.0 2.0 constant_dynamic-slice_fusion.10
  148.5 1.5 fusion.258
  150.0 1.3 convolution_add_fusion.24
  151.3 1.3 convolution_add_fusion.25
  155.8 1.5 reshape.142
  166.8 1.9 copy-done.1
  169.6 2.0 constant_dynamic-slice_fusion.10
  172.1 1.5 fusion.258
  173.6 1.3 convolution_add_fusion.24
  175.0 1.3 convolution_add_fusion.25
  179.4 1.5 reshape.142
  190.5 1.9 copy-done.1
  193.3 2.0 constant_dynamic-slice_fusion.10
  195.8 1.5 fusion.258
  197.3 1.3 convolution_add_fusion.24
  198.6 1.3 convolution_add_fusion.25
  203.1 1.5 reshape.142
  214.1 1.9 copy-done.1
  216.0 4.4 %broadcast_multiply_fusion = f32[10368,96]{0,1:T(8,128)} fusion(f32[10368,96]{0,1:T(8,128)} %get-tuple-element.159), kind=kLoop, calls=%fused_computation.81 | loop fusion | flops 995328 | bytes 7962624 | tf_op jit(solution)/shard_map/mul | solution.py:146
  220.4 5.9 %copy.39 = f32[10368,96]{1,0:T(8,128)} copy(f32[10368,96]{0,1:T(8,128)} %broadcast_multiply_fusion) | data formatting | bytes 7962624
  226.4 3.6 %all-to-all-start.1 = ((f32[1,8,160,96]{3,2,0,1:T(8,128)}), f32[1,8,160,96]{3,2,0,1:T(8,128)S(1)}, u32[]{:S(2)}, u32[]{:S(2)}) async-start(f32[1,8,160,96]{3,2,0,1:T(8,128)} %bitcast.6), calls=%async_computation.1 | async-start | bytes 1310720 | tf_op jit(solution)/shard_map/all_to_all | solution.py:148
  230.1 10.2 %all-to-all-done.1 = f32[1,8,160,96]{3,2,0,1:T(8,128)S(1)} async-done(((f32[1,8,160,96]{3,2,0,1:T(8,128)}), f32[1,8,160,96]{3,2,0,1:T(8,128)S(1)}, u32[]{:S(2)}, u32[]{:S(2)}) %all-to-all-start.1) | async-done | bytes 491552 | tf_op jit(solution)/shard_map/all_to_all | solution.py:148
  242.1 81.2 %reduce-scatter.4.cloned.1.call-done = f32[2592,96]{1,0:T(8,128)} async-done(((f32[10368,96]{1,0:T(8,128)}), f32[2592,96]{1,0:T(8,128)}) %reduce-scatter.4.cloned.1.call-update) | async-done | bytes 995344
  323.3 2.7 copy.40
  (301 shorter events, 74.5 us)
Async XLA Ops:
  7.2 108.5 %all-gather.2.cloned.1.call-start = ((), (), s32[]{:S(2)}) async-start(), calls=%async_computation.3 | async-start | bytes 3686400 | tf_op jit(solution)/shard_map/all_gather | solution.py:124
  8.2 3.7 %collective-permute-start.2 = (bf16[1,1,160,384]{3,2,1,0:T(8,128)(2,1)S(1)}, bf16[1,1,160,384]{3,2,1,0:T(8,128)(2,1)S(1)}, u32[]{:S(2)}, u32[]{:S(2)}) collective-permute-start(bf16[1,1,160,384]{3,2,1,0:T(8,128)(2,1)S(1)} %get-tuple-element.244), channel_id=1, source_target_pairs={{0,1},{1,2},{2,3},{4,5},{5,6},{6,7},{8,9},{9,10},{10,11},{12,13},{... | collective-permute-start | bytes 368648 | tf_op jit(solution)/shard_map/ppermute | solution.py:22
  10.6 5.3 %collective-permute-start.3 = (bf16[1,1,160,384]{3,2,1,0:T(8,128)(2,1)S(1)}, bf16[1,1,160,384]{3,2,1,0:T(8,128)(2,1)S(1)}, u32[]{:S(2)}, u32[]{:S(2)}) collective-permute-start(bf16[1,1,160,384]{3,2,1,0:T(8,128)(2,1)S(1)} %get-tuple-element.243), channel_id=1, source_target_pairs={{1,0},{2,1},{3,2},{5,4},{6,5},{7,6},{9,8},{10,9},{11,10},{13,12},{... | collective-permute-start | bytes 368648 | tf_op jit(solution)/shard_map/ppermute | solution.py:24
  15.9 26.2 %collective-permute-start.5 = (bf16[1,4,160,384]{3,2,1,0:T(8,128)(2,1)S(1)}, bf16[1,4,160,384]{3,2,1,0:T(8,128)(2,1)S(1)}, u32[]{:S(2)}, u32[]{:S(2)}) collective-permute-start(bf16[1,4,160,384]{3,2,1,0:T(8,128)(2,1)S(1)} %constant_dynamic-update-slice_fusion.1), channel_id=1, source_target_pairs={{8,0},{12,4},{9,1},{13,5},{10,2},{14,6},{11,3},{15,7},{24,16},{28,... | collective-permute-start | bytes 1474568 | tf_op jit(solution)/shard_map/ppermute | solution.py:11
  17.2 24.9 %collective-permute-start.4 = (bf16[1,4,160,384]{3,2,1,0:T(8,128)(2,1)S(1)}, bf16[1,4,160,384]{3,2,1,0:T(8,128)(2,1)S(1)}, u32[]{:S(2)}, u32[]{:S(2)}) collective-permute-start(bf16[1,4,160,384]{3,2,1,0:T(8,128)(2,1)S(1)} %constant_dynamic-update-slice_fusion.1), channel_id=1, source_target_pairs={{4,0},{8,4},{12,8},{5,1},{9,5},{13,9},{6,2},{10,6},{14,10},{7,3},{... | collective-permute-start | bytes 1474568 | tf_op jit(solution)/shard_map/ppermute | solution.py:11
  43.4 7.6 %slice-start = ((s8[7962624]{0:T(1024)(128)(4,1)}), s8[4194304]{0:T(1024)(128)(4,1)S(1)}, s32[]{:S(2)}) async-start(s8[7962624]{0:T(1024)(128)(4,1)} %bitcast.311), calls=%async_computation.5 | async-start | bytes 8388608
  47.1 3.8 %slice-start.1 = ((s8[7962624]{0:T(1024)(128)(4,1)}), s8[3768320]{0:T(1024)(128)(4,1)S(1)}, s32[]{:S(2)}) async-start(s8[7962624]{0:T(1024)(128)(4,1)} %bitcast.311), calls=%async_computation.6 | async-start | bytes 7536640
  54.2 1.7 copy-start.10
  54.8 28.8 %copy-start.3 = (bf16[1,2,160,384]{3,2,1,0:T(8,128)(2,1)S(1)}, bf16[1,2,160,384]{3,2,1,0:T(8,128)(2,1)}, u32[]{:S(2)}) copy-start(bf16[1,2,160,384]{3,2,1,0:T(8,128)(2,1)} %param.11) | copy-start | bytes 737284
  58.0 19.3 %collective-permute-start.1 = (bf16[1,2,160,384]{3,2,1,0:T(8,128)(2,1)S(1)}, bf16[1,2,160,384]{3,2,1,0:T(8,128)(2,1)S(1)}, u32[]{:S(2)}, u32[]{:S(2)}) collective-permute-start(bf16[1,2,160,384]{3,2,1,0:T(8,128)(2,1)S(1)} %get-tuple-element.240), channel_id=1, source_target_pairs={{0,4},{4,8},{8,12},{1,5},{5,9},{9,13},{2,6},{6,10},{10,14},{3,7},{... | collective-permute-start | bytes 737288 | tf_op jit(solution)/shard_map/ppermute | solution.py:11
  71.0 11.6 %collective-permute-start = (bf16[1,2,160,384]{3,2,1,0:T(8,128)(2,1)S(1)}, bf16[1,2,160,384]{3,2,1,0:T(8,128)(2,1)S(1)}, u32[]{:S(2)}, u32[]{:S(2)}) collective-permute-start(bf16[1,2,160,384]{3,2,1,0:T(8,128)(2,1)S(1)} %get-tuple-element.240), channel_id=1, source_target_pairs={{0,8},{4,12},{1,9},{5,13},{2,10},{6,14},{3,11},{7,15},{16,24},{20,... | collective-permute-start | bytes 737288 | tf_op jit(solution)/shard_map/ppermute | solution.py:11
  84.8 14.0 %all-to-all-start = ((bf16[1,2,160,384]{2,1,0,3:T(2,128)(2,1)}), bf16[1,2,160,384]{2,1,0,3:T(2,128)(2,1)S(1)}, u32[]{:S(2)}, u32[]{:S(2)}) async-start(bf16[1,2,160,384]{2,1,0,3:T(2,128)(2,1)} %copy.31), calls=%async_computation | async-start | bytes 786432 | tf_op jit(solution)/shard_map/all_to_all | solution.py:104
  88.2 235.0 %reduce-scatter.4.cloned.1.call-start = ((), (), s32[]{:S(2)}) async-start(), calls=%async_computation.4 | async-start | bytes 6635520
  121.4 0.8 copy-start.7
  124.8 4.2 %copy-start.2 = (bf16[9,384,288]{2,1,0:T(8,128)(2,1)S(1)}, bf16[9,384,288]{2,1,0:T(8,128)(2,1)}, u32[]{:S(2)}) copy-start(bf16[9,384,288]{2,1,0:T(8,128)(2,1)} %get-tuple-element.336) | copy-start | bytes 5971972 | tf_op jit(solution)/shard_map/while
  137.8 4.3 %copy-start = (f32[10368,96]{0,1:T(8,128)S(1)}, f32[10368,96]{0,1:T(8,128)}, u32[]{:S(2)}) copy-start(f32[10368,96]{0,1:T(8,128)} %get-tuple-element.321) | copy-start | bytes 11943940 | tf_op jit(solution)/shard_map/while
  142.1 2.9 copy-start.8
  143.1 1.9 copy-start.1
  145.0 0.8 copy-start.7
  148.5 4.2 %copy-start.2 = (bf16[9,384,288]{2,1,0:T(8,128)(2,1)S(1)}, bf16[9,384,288]{2,1,0:T(8,128)(2,1)}, u32[]{:S(2)}) copy-start(bf16[9,384,288]{2,1,0:T(8,128)(2,1)} %get-tuple-element.336) | copy-start | bytes 5971972 | tf_op jit(solution)/shard_map/while
  161.5 4.3 %copy-start = (f32[10368,96]{0,1:T(8,128)S(1)}, f32[10368,96]{0,1:T(8,128)}, u32[]{:S(2)}) copy-start(f32[10368,96]{0,1:T(8,128)} %get-tuple-element.321) | copy-start | bytes 11943940 | tf_op jit(solution)/shard_map/while
  165.8 2.9 copy-start.8
  166.8 1.9 copy-start.1
  168.7 0.8 copy-start.7
  172.1 4.2 %copy-start.2 = (bf16[9,384,288]{2,1,0:T(8,128)(2,1)S(1)}, bf16[9,384,288]{2,1,0:T(8,128)(2,1)}, u32[]{:S(2)}) copy-start(bf16[9,384,288]{2,1,0:T(8,128)(2,1)} %get-tuple-element.336) | copy-start | bytes 5971972 | tf_op jit(solution)/shard_map/while
  185.1 4.3 %copy-start = (f32[10368,96]{0,1:T(8,128)S(1)}, f32[10368,96]{0,1:T(8,128)}, u32[]{:S(2)}) copy-start(f32[10368,96]{0,1:T(8,128)} %get-tuple-element.321) | copy-start | bytes 11943940 | tf_op jit(solution)/shard_map/while
  189.4 2.9 copy-start.8
  190.5 1.9 copy-start.1
  192.4 0.8 copy-start.7
  195.8 4.2 %copy-start.2 = (bf16[9,384,288]{2,1,0:T(8,128)(2,1)S(1)}, bf16[9,384,288]{2,1,0:T(8,128)(2,1)}, u32[]{:S(2)}) copy-start(bf16[9,384,288]{2,1,0:T(8,128)(2,1)} %get-tuple-element.336) | copy-start | bytes 5971972 | tf_op jit(solution)/shard_map/while
  208.8 4.3 %copy-start = (f32[10368,96]{0,1:T(8,128)S(1)}, f32[10368,96]{0,1:T(8,128)}, u32[]{:S(2)}) copy-start(f32[10368,96]{0,1:T(8,128)} %get-tuple-element.321) | copy-start | bytes 11943940 | tf_op jit(solution)/shard_map/while
  213.1 2.9 copy-start.8
  214.1 1.9 copy-start.1
  226.4 14.6 %copy-start.4 = (bf16[1,2,160,384]{3,2,1,0:T(8,128)(2,1)S(1)}, bf16[1,2,160,384]{3,2,1,0:T(8,128)(2,1)}, u32[]{:S(2)}) copy-start(bf16[1,2,160,384]{3,2,1,0:T(8,128)(2,1)} %param.11) | copy-start | bytes 737284
  226.4 14.7 %copy-start.5 = (bf16[1,2,160,384]{3,2,1,0:T(8,128)(2,1)S(1)}, bf16[1,2,160,384]{3,2,1,0:T(8,128)(2,1)}, u32[]{:S(2)}) copy-start(bf16[1,2,160,384]{3,2,1,0:T(8,128)(2,1)} %param.7) | copy-start | bytes 737284
  226.4 14.7 %copy-start.6 = (f32[1,2,160,384]{3,2,1,0:T(8,128)S(1)}, f32[1,2,160,384]{3,2,1,0:T(8,128)}, u32[]{:S(2)}) copy-start(f32[1,2,160,384]{3,2,1,0:T(8,128)} %get-tuple-element.215) | copy-start | bytes 1474564
  226.4 14.7 %copy-start.9 = (f32[384]{0:T(512)S(1)}, f32[384]{0:T(512)}, u32[]{:S(2)}) copy-start(f32[384]{0:T(512)} %param.9) | copy-start | bytes 4612
  226.4 13.9 %all-to-all-start.1 = ((f32[1,8,160,96]{3,2,0,1:T(8,128)}), f32[1,8,160,96]{3,2,0,1:T(8,128)S(1)}, u32[]{:S(2)}, u32[]{:S(2)}) async-start(f32[1,8,160,96]{3,2,0,1:T(8,128)} %bitcast.6), calls=%async_computation.1 | async-start | bytes 1310720 | tf_op jit(solution)/shard_map/all_to_all | solution.py:148
Sparse Core Ops, SparseCore 0:
  83.7 31.9 all-gather.1
  226.5 96.6 reduce-scatter.3
where the time goes:
time: 334 us; the launch traced here: 333 us
  waiting for transfers between devices  144 us (43%)
  matrix products  67.3 us (20%)
  local copies, waits for them, and re-layouts  61.8 us (19%)
  starting transfers between devices  27.7 us (8%)
  other arithmetic  16 us (5%)
  between operations  14.4 us (4%)
    unnamed x3, waiting for transfers between devices  81.2 us
    ppermute x4, waiting for transfers between devices, shifted_2(): return lax.ppermute(value, axis, pairs)  32.8 us
    dot_general x36, matrix products, forward_sum(): jnp.dot(slab, arranged[3 * depth_tap + row_tap], preferred_element_type=j...  28.8 us
    dot_general x108, matrix products, weight_terms(): lax.dot_general(slab, shifted[col_tap], (((0,), (0,)), ((), ())), preferr...  27.8 us
    ppermute x4, starting transfers between devices, shifted_2(): return lax.ppermute(value, axis, pairs)  16.9 us
    all_gather x1, waiting for transfers between devices, local(): gathered = lax.all_gather(stacked, 'height', axis=1, tiled=True)  16.5 us
    unnamed x22, local copies, waits for them, and re-layouts  15.2 us
    dot_general x9, matrix products, backward_sum(): jnp.dot(slab, arranged[3 * depth_tap + row_tap], preferred_element_type=j...  10.7 us
  transfers between devices with their start and end apart: 10, of which 7 were waited for; matrix products, arithmetic and copies ran while one was open for 5% of the time, Pallas kernels for 0%

commit v1 on v0

--- a/solution.py
+++ b/solution.py
@@ -121,7 +121,14 @@
     prior = shifted_2(hidden, "tm", 1)
     second = shifted_2(hidden, "tm", 2)
     stacked = jnp.concatenate([second, prior, hidden], axis=0)
-    gathered = lax.all_gather(stacked, "height", axis=1, tiled=True)
+    ring = [stacked]
+    for hop in range(3):
+        ring.append(lax.ppermute(ring[-1], "height", [(dev, (dev + 1) % 4) for dev in range(4)]))
+    gathered = jnp.roll(
+        jnp.concatenate(ring[::-1], axis=1),
+        (lax.axis_index("height") + 1) * ring[0].shape[1],
+        axis=1,
+    )
     framed = jnp.pad(gathered, ((0, 0), (1, 1), (1, 1), (0, 0)))
     shared_cot = column_share(cotangent)
     share_cube = lax.dynamic_slice_in_dim(weight_cube, first_column, share_width, 4)

time: 334 us -> 478 us (1.43)
  matrix products: 67.3 us -> 157 us
  local copies, waits for them, and re-layouts: 61.8 us -> 89.2 us
  other arithmetic: 16 us -> 32.2 us
  waiting for transfers between devices: 144 us -> 153 us
    dot_general x108, matrix products: 27.8 us -> 101 us  [weight_terms(): lax.dot_general(slab, shifted[col_tap], (((0,), (0,)), ((), ())), preferr...]
    ppermute x0 -> x3, waiting for transfers between devices: none -> 21.7 us  [local(): lax.ppermute(ring[-1], 'height', [(dev, (dev + 1) % 4) for dev in range(4)])]
    squeeze x36, local copies, waits for them, and re-layouts: 1.93 us -> 21.3 us  [forward_sum(): window[depth_tap, row_tap:row_tap + row_total]]
    add x4, other arithmetic: 4.1 us -> 21.8 us  [block_step(): grad_total + weight_terms(window, cot_block, row_count, col_count)]
    all_gather x1 -> x0, waiting for transfers between devices: 16.5 us -> none  [local(): gathered = lax.all_gather(stacked, 'height', axis=1, tiled=True)]
    dot_general x36, matrix products: 28.8 us -> 43.9 us  [forward_sum(): jnp.dot(slab, arranged[3 * depth_tap + row_tap], preferred_element_type=j...]
    while x40, local copies, waits for them, and re-layouts: 10.6 us -> 0.08 us
    slice x4, local copies, waits for them, and re-layouts: 7.89 us -> 16 us  [forward_sum(): window[depth_tap, row_tap:row_tap + row_total]]
  transfers between devices with their start and end apart: 10 -> 12, of which waited for: 7 -> 8; matrix products, arithmetic and copies ran while one was open for 5% -> 3% of each run, Pallas kernels for 0% -> 0%
where the time goes in v1:
time: 478 us; the launch traced here: 475 us
  matrix products  157 us (33%)
  waiting for transfers between devices  153 us (32%)
  local copies, waits for them, and re-layouts  89.2 us (19%)
  other arithmetic  32.2 us (7%)
  starting transfers between devices  28.8 us (6%)
  between operations  14.5 us (3%)
    dot_general x108, matrix products, weight_terms(): lax.dot_general(slab, shifted[col_tap], (((0,), (0,)), ((), ())), preferr...  101 us
    unnamed x2, waiting for transfers between devices  85 us
    dot_general x36, matrix products, forward_sum(): jnp.dot(slab, arranged[3 * depth_tap + row_tap], preferred_element_type=j...  43.9 us
    ppermute x4, waiting for transfers between devices, shifted_2(): return lax.ppermute(value, axis, pairs)  32.8 us
    add x4, other arithmetic, block_step(): grad_total + weight_terms(window, cot_block, row_count, col_count)  21.8 us
    ppermute x3, waiting for transfers between devices, local(): lax.ppermute(ring[-1], 'height', [(dev, (dev + 1) % 4) for dev in range(4)])  21.7 us
    squeeze x36, local copies, waits for them, and re-layouts, forward_sum(): window[depth_tap, row_tap:row_tap + row_total]  21.3 us
    unnamed x34, local copies, waits for them, and re-layouts  20.3 us
  transfers between devices with their start and end apart: 12, of which 8 were waited for; matrix products, arithmetic and copies ran while one was open for 3% of the time, Pallas kernels for 0%

profile of v1, /device:TPU:0, one launch (start us, length us, event | category | flops | bytes accessed | tf_op | source)
XLA Modules:
  0.0 475.1 jit_solution(16146416434552156268)
XLA Ops:
  8.2 2.4 collective-permute-start.5
  12.8 3.0 collective-permute-done.6
  19.6 22.5 %collective-permute-done.8 = bf16[1,4,160,384]{3,2,1,0:T(8,128)(2,1)S(1)} collective-permute-done((bf16[1,4,160,384]{3,2,1,0:T(8,128)(2,1)S(1)}, bf16[1,4,160,384]{3,2,1,0:T(8,128)(2,1)S(1)}, u32[]{:S(2)}, u32[]{:S(2)}) %collective-permute-start.8) | collective-permute-done | bytes 491552 | tf_op jit(solution)/shard_map/ppermute | solution.py:11
  44.5 1.7 reshape_squeeze.28
  47.3 1.9 fusion.26
  49.3 1.9 convolution_add_fusion.15
  51.2 2.1 convolution_add_fusion.14
  53.3 1.8 convolution_add_fusion.13
  57.7 1.8 convolution_add_fusion.8
  59.5 2.5 reshape.131
  64.2 13.0 %collective-permute-start.1 = (bf16[1,2,160,384]{3,2,1,0:T(8,128)(2,1)S(1)}, bf16[1,2,160,384]{3,2,1,0:T(8,128)(2,1)S(1)}, u32[]{:S(2)}, u32[]{:S(2)}) collective-permute-start(bf16[1,2,160,384]{3,2,1,0:T(8,128)(2,1)S(1)} %get-tuple-element.240), channel_id=1, source_target_pairs={{0,4},{4,8},{8,12},{1,5},{5,9},{9,13},{2,6},{6,10},{10,14},{3,7},{... | collective-permute-start | bytes 737288 | tf_op jit(solution)/shard_map/ppermute | solution.py:11
  78.6 5.0 %collective-permute-done.1 = bf16[1,2,160,384]{3,2,1,0:T(8,128)(2,1)S(1)} collective-permute-done((bf16[1,2,160,384]{3,2,1,0:T(8,128)(2,1)S(1)}, bf16[1,2,160,384]{3,2,1,0:T(8,128)(2,1)S(1)}, u32[]{:S(2)}, u32[]{:S(2)}) %collective-permute-start.1) | collective-permute-done | bytes 245792 | tf_op jit(solution)/shard_map/ppermute | solution.py:11
  83.5 5.3 %collective-permute-done = bf16[1,2,160,384]{3,2,1,0:T(8,128)(2,1)S(1)} collective-permute-done((bf16[1,2,160,384]{3,2,1,0:T(8,128)(2,1)S(1)}, bf16[1,2,160,384]{3,2,1,0:T(8,128)(2,1)S(1)}, u32[]{:S(2)}, u32[]{:S(2)}) %collective-permute-start) | collective-permute-done | bytes 245792 | tf_op jit(solution)/shard_map/ppermute | solution.py:11
  89.2 10.7 %collective-permute-done.2 = bf16[3,2,160,384]{3,2,1,0:T(8,128)(2,1)S(1)} collective-permute-done((bf16[3,2,160,384]{3,2,1,0:T(8,128)(2,1)S(1)}, bf16[3,2,160,384]{3,2,1,0:T(8,128)(2,1)S(1)}, u32[]{:S(2)}, u32[]{:S(2)}) %collective-permute-start.2) | collective-permute-done | bytes 737312 | tf_op jit(solution)/shard_map/ppermute | solution.py:126
  99.9 11.0 %collective-permute-done.3 = bf16[3,2,160,384]{3,2,1,0:T(8,128)(2,1)} collective-permute-done((bf16[3,2,160,384]{3,2,1,0:T(8,128)(2,1)S(1)}, bf16[3,2,160,384]{3,2,1,0:T(8,128)(2,1)}, u32[]{:S(2)}, u32[]{:S(2)}) %collective-permute-start.3) | collective-permute-done | bytes 737312 | tf_op jit(solution)/shard_map/ppermute | solution.py:126
  112.0 4.1 all-to-all-start
  116.4 3.5 dynamic-slice_bitcast_fusion.1
  119.9 2.4 copy.30
  122.4 3.0 copy.33
  125.4 1.9 copy.32
  134.4 3.2 pad.41
  138.5 216.1 %while.18 = (s32[]{:T(128)}, f32[8,160,96]{2,1,0:T(8,128)}, f32[10368,96]{0,1:T(8,128)}, bf16[3,10,162,384]{3,2,1,0:T(8,128)(2,1)}, bf16[9,384,288]{2,1,0:T(8,12...) while((s32[]{:T(128)}, f32[8,160,96]{2,1,0:T(8,128)}, ...), condition=%wide.region_2.3_spmd.clone, body=%wide.region_1.2_spmd.clone.sunk | while | flops 1292743680 | bytes 65949612 | solution.py:151
  138.5 4.0 constant_dynamic-slice_fusion.11
  144.0 1.3 convolution_add_fusion.24
  147.8 1.3 convolution_add_fusion.26
  151.5 1.3 convolution_add_fusion.28
  155.3 1.3 convolution_add_fusion.30
  187.0 4.6 select_add_fusion.2
  191.6 4.0 constant_dynamic-slice_fusion.11
  197.1 1.3 convolution_add_fusion.24
  200.9 1.3 convolution_add_fusion.26
  204.7 1.3 convolution_add_fusion.28
  240.1 5.8 %select_add_fusion.2 = f32[10368,96]{0,1:T(8,128)} fusion(f32[10368,96]{0,1:T(8,128)} %convolution_dynamic-update-slice_fusion.80, f32[10368,96]{0,1:T(8,128)} %get-tuple-element.321, pred[]{:T(512)S(6)} %compare.49), kind=kLoop, calls=%fused_computation.clone.1 | loop fusion | flops 1990656 | bytes 11943937 | tf_op jit(solution)/shard_map/while/body/eval_jaxpr/add | solution.py:144
  245.9 4.0 constant_dynamic-slice_fusion.11
  251.4 1.3 convolution_add_fusion.24
  255.2 1.3 convolution_add_fusion.26
  259.0 1.3 convolution_add_fusion.28
  294.5 5.8 %select_add_fusion.2 = f32[10368,96]{0,1:T(8,128)} fusion(f32[10368,96]{0,1:T(8,128)} %convolution_dynamic-update-slice_fusion.80, f32[10368,96]{0,1:T(8,128)} %get-tuple-element.321, pred[]{:T(512)S(6)} %compare.49), kind=kLoop, calls=%fused_computation.clone.1 | loop fusion | flops 1990656 | bytes 11943937 | tf_op jit(solution)/shard_map/while/body/eval_jaxpr/add | solution.py:144
  300.2 4.0 constant_dynamic-slice_fusion.11
  305.7 1.3 convolution_add_fusion.24
  309.6 1.3 convolution_add_fusion.26
  348.8 5.8 %select_add_fusion.2 = f32[10368,96]{0,1:T(8,128)} fusion(f32[10368,96]{0,1:T(8,128)} %convolution_dynamic-update-slice_fusion.80, f32[10368,96]{0,1:T(8,128)} %get-tuple-element.321, pred[]{:T(512)S(6)} %compare.49), kind=kLoop, calls=%fused_computation.clone.1 | loop fusion | flops 1990656 | bytes 11943937 | tf_op jit(solution)/shard_map/while/body/eval_jaxpr/add | solution.py:144
  354.5 4.4 broadcast_multiply_fusion
  359.0 5.9 %copy.39 = f32[10368,96]{1,0:T(8,128)} copy(f32[10368,96]{0,1:T(8,128)} %broadcast_multiply_fusion) | data formatting | bytes 7962624
  364.9 3.6 all-to-all-start.1
  368.6 10.2 %all-to-all-done.1 = f32[1,8,160,96]{3,2,0,1:T(8,128)S(1)} async-done(((f32[1,8,160,96]{3,2,0,1:T(8,128)}), f32[1,8,160,96]{3,2,0,1:T(8,128)S(1)}, u32[]{:S(2)}, u32[]{:S(2)}) %all-to-all-start.1) | async-done | bytes 491552 | tf_op jit(solution)/shard_map/all_to_all | solution.py:155
  380.6 85.0 %reduce-scatter.4.cloned.1.call-done = f32[2592,96]{1,0:T(8,128)} async-done(((f32[10368,96]{1,0:T(8,128)}), f32[2592,96]{1,0:T(8,128)}) %reduce-scatter.4.cloned.1.call-update) | async-done | bytes 995344
  465.6 2.7 copy.40
  (319 shorter events, 189.3 us)
Async XLA Ops:
  8.2 3.7 collective-permute-start.5
  10.5 5.3 %collective-permute-start.6 = (bf16[1,1,160,384]{3,2,1,0:T(8,128)(2,1)S(1)}, bf16[1,1,160,384]{3,2,1,0:T(8,128)(2,1)S(1)}, u32[]{:S(2)}, u32[]{:S(2)}) collective-permute-start(bf16[1,1,160,384]{3,2,1,0:T(8,128)(2,1)S(1)} %get-tuple-element.243), channel_id=1, source_target_pairs={{1,0},{2,1},{3,2},{5,4},{6,5},{7,6},{9,8},{10,9},{11,10},{13,12},{... | collective-permute-start | bytes 368648 | tf_op jit(solution)/shard_map/ppermute | solution.py:24
  15.9 26.2 %collective-permute-start.8 = (bf16[1,4,160,384]{3,2,1,0:T(8,128)(2,1)S(1)}, bf16[1,4,160,384]{3,2,1,0:T(8,128)(2,1)S(1)}, u32[]{:S(2)}, u32[]{:S(2)}) collective-permute-start(bf16[1,4,160,384]{3,2,1,0:T(8,128)(2,1)S(1)} %constant_dynamic-update-slice_fusion.9), channel_id=1, source_target_pairs={{8,0},{12,4},{9,1},{13,5},{10,2},{14,6},{11,3},{15,7},{24,16},{28,... | collective-permute-start | bytes 1474568 | tf_op jit(solution)/shard_map/ppermute | solution.py:11
  17.2 24.9 %collective-permute-start.7 = (bf16[1,4,160,384]{3,2,1,0:T(8,128)(2,1)S(1)}, bf16[1,4,160,384]{3,2,1,0:T(8,128)(2,1)S(1)}, u32[]{:S(2)}, u32[]{:S(2)}) collective-permute-start(bf16[1,4,160,384]{3,2,1,0:T(8,128)(2,1)S(1)} %constant_dynamic-update-slice_fusion.9), channel_id=1, source_target_pairs={{4,0},{8,4},{12,8},{5,1},{9,5},{13,9},{6,2},{10,6},{14,10},{7,3},{... | collective-permute-start | bytes 1474568 | tf_op jit(solution)/shard_map/ppermute | solution.py:11
  47.3 7.8 %slice-start = ((s8[7962624]{0:T(1024)(128)(4,1)}), s8[4194304]{0:T(1024)(128)(4,1)S(1)}, s32[]{:S(2)}) async-start(s8[7962624]{0:T(1024)(128)(4,1)} %bitcast.311), calls=%async_computation.4 | async-start | bytes 8388608
  51.2 3.9 slice-start.1
  59.5 3.5 copy-start.9
  59.5 3.5 copy-start.13
  62.0 48.9 %copy-start.5 = (bf16[1,2,160,384]{3,2,1,0:T(8,128)(2,1)S(1)}, bf16[1,2,160,384]{3,2,1,0:T(8,128)(2,1)}, u32[]{:S(2)}) copy-start(bf16[1,2,160,384]{3,2,1,0:T(8,128)(2,1)} %param.11) | copy-start | bytes 737284
  64.2 19.3 %collective-permute-start.1 = (bf16[1,2,160,384]{3,2,1,0:T(8,128)(2,1)S(1)}, bf16[1,2,160,384]{3,2,1,0:T(8,128)(2,1)S(1)}, u32[]{:S(2)}, u32[]{:S(2)}) collective-permute-start(bf16[1,2,160,384]{3,2,1,0:T(8,128)(2,1)S(1)} %get-tuple-element.240), channel_id=1, source_target_pairs={{0,4},{4,8},{8,12},{1,5},{5,9},{9,13},{2,6},{6,10},{10,14},{3,7},{... | collective-permute-start | bytes 737288 | tf_op jit(solution)/shard_map/ppermute | solution.py:11
  77.2 11.6 %collective-permute-start = (bf16[1,2,160,384]{3,2,1,0:T(8,128)(2,1)S(1)}, bf16[1,2,160,384]{3,2,1,0:T(8,128)(2,1)S(1)}, u32[]{:S(2)}, u32[]{:S(2)}) collective-permute-start(bf16[1,2,160,384]{3,2,1,0:T(8,128)(2,1)S(1)} %get-tuple-element.240), channel_id=1, source_target_pairs={{0,8},{4,12},{1,9},{5,13},{2,10},{6,14},{3,11},{7,15},{16,24},{20,... | collective-permute-start | bytes 737288 | tf_op jit(solution)/shard_map/ppermute | solution.py:11
  88.9 10.9 %collective-permute-start.2 = (bf16[3,2,160,384]{3,2,1,0:T(8,128)(2,1)S(1)}, bf16[3,2,160,384]{3,2,1,0:T(8,128)(2,1)S(1)}, u32[]{:S(2)}, u32[]{:S(2)}) collective-permute-start(bf16[3,2,160,384]{3,2,1,0:T(8,128)(2,1)S(1)} %pad_maximum_fusion), channel_id=1, source_target_pairs={{0,1},{1,2},{2,3},{3,0},{4,5},{5,6},{6,7},{7,4},{8,9},{9,10},{10,1... | collective-permute-start | bytes 2211848 | tf_op jit(solution)/shard_map/ppermute | solution.py:126
  99.9 16.6 %copy-start.7 = (bf16[3,2,160,384]{3,2,1,0:T(8,128)(2,1)}, bf16[3,2,160,384]{3,2,1,0:T(8,128)(2,1)S(1)}, u32[]{:S(2)}) copy-start(bf16[3,2,160,384]{3,2,1,0:T(8,128)(2,1)S(1)} %collective-permute-done.2) | copy-start | bytes 2211844
  99.9 11.0 %collective-permute-start.3 = (bf16[3,2,160,384]{3,2,1,0:T(8,128)(2,1)S(1)}, bf16[3,2,160,384]{3,2,1,0:T(8,128)(2,1)}, u32[]{:S(2)}, u32[]{:S(2)}) collective-permute-start(bf16[3,2,160,384]{3,2,1,0:T(8,128)(2,1)S(1)} %collective-permute-done.2), channel_id=1, source_target_pairs={{0,1},{1,2},{2,3},{3,0},{4,5},{5,6},{6,7},{7,4},{8,9},{9,10},{10,1... | collective-permute-start | bytes 2211848 | tf_op jit(solution)/shard_map/ppermute | solution.py:126
  110.9 16.4 %collective-permute-start.4 = (bf16[3,2,160,384]{3,2,1,0:T(8,128)(2,1)}, bf16[3,2,160,384]{3,2,1,0:T(8,128)(2,1)}, u32[]{:S(2)}, u32[]{:S(2)}) collective-permute-start(bf16[3,2,160,384]{3,2,1,0:T(8,128)(2,1)} %collective-permute-done.3), channel_id=1, source_target_pairs={{0,1},{1,2},{2,3},{3,0},{4,5},{5,6},{6,7},{7,4},{8,9},{9,10},{10,1... | collective-permute-start | bytes 2211848 | tf_op jit(solution)/shard_map/ppermute | solution.py:126
  112.0 13.3 %all-to-all-start = ((bf16[1,2,160,384]{2,1,0,3:T(2,128)(2,1)}), bf16[1,2,160,384]{2,1,0,3:T(2,128)(2,1)}, u32[]{:S(2)}, u32[]{:S(2)}) async-start(bf16[1,2,160,384]{2,1,0,3:T(2,128)(2,1)} %copy.31), calls=%async_computation | async-start | bytes 786432 | tf_op jit(solution)/shard_map/all_to_all | solution.py:104
  116.2 349.4 %reduce-scatter.4.cloned.1.call-start = ((), (), s32[]{:S(2)}) async-start(), calls=%async_computation.3 | async-start | bytes 6635520
  128.5 5.2 %copy-start.8 = (bf16[3,2,160,384]{3,2,1,0:T(8,128)(2,1)S(1)}, bf16[3,2,160,384]{3,2,1,0:T(8,128)(2,1)}, u32[]{:S(2)}) copy-start(bf16[3,2,160,384]{3,2,1,0:T(8,128)(2,1)} %copy-done.7) | copy-start | bytes 2211844
  138.5 4.4 copy-start
  142.9 4.8 %copy-start.4 = (bf16[1,2,162,384]{3,2,1,0:T(8,128)(2,1)S(1)}, bf16[1,2,162,384]{3,2,1,0:T(8,128)(2,1)}, u32[]{:S(2)}) copy-start(bf16[1,2,162,384]{3,2,1,0:T(8,128)(2,1)} %get-tuple-element.297) | copy-start | bytes 746500 | tf_op jit(solution)/shard_map/while
  145.3 3.8 copy-start.3
  145.3 7.5 %copy-start.2 = (bf16[1,2,162,384]{3,2,1,0:T(8,128)(2,1)S(1)}, bf16[1,2,162,384]{3,2,1,0:T(8,128)(2,1)}, u32[]{:S(2)}) copy-start(bf16[1,2,162,384]{3,2,1,0:T(8,128)(2,1)} %get-tuple-element.300) | copy-start | bytes 746500 | tf_op jit(solution)/shard_map/while
  187.0 4.6 copy-start.1
  191.6 4.5 copy-start
  196.1 4.8 %copy-start.4 = (bf16[1,2,162,384]{3,2,1,0:T(8,128)(2,1)S(1)}, bf16[1,2,162,384]{3,2,1,0:T(8,128)(2,1)}, u32[]{:S(2)}) copy-start(bf16[1,2,162,384]{3,2,1,0:T(8,128)(2,1)} %get-tuple-element.297) | copy-start | bytes 746500 | tf_op jit(solution)/shard_map/while
  198.4 3.8 copy-start.3
  198.5 7.5 %copy-start.2 = (bf16[1,2,162,384]{3,2,1,0:T(8,128)(2,1)S(1)}, bf16[1,2,162,384]{3,2,1,0:T(8,128)(2,1)}, u32[]{:S(2)}) copy-start(bf16[1,2,162,384]{3,2,1,0:T(8,128)(2,1)} %get-tuple-element.300) | copy-start | bytes 746500 | tf_op jit(solution)/shard_map/while
  240.1 5.8 %copy-start.1 = (bf16[9,384,288]{2,1,0:T(8,128)(2,1)S(1)}, bf16[9,384,288]{2,1,0:T(8,128)(2,1)}, u32[]{:S(2)}) copy-start(bf16[9,384,288]{2,1,0:T(8,128)(2,1)} %copy-done) | copy-start | bytes 5971972 | tf_op jit(solution)/shard_map/while
  245.9 4.5 copy-start
  250.4 4.8 %copy-start.4 = (bf16[1,2,162,384]{3,2,1,0:T(8,128)(2,1)S(1)}, bf16[1,2,162,384]{3,2,1,0:T(8,128)(2,1)}, u32[]{:S(2)}) copy-start(bf16[1,2,162,384]{3,2,1,0:T(8,128)(2,1)} %get-tuple-element.297) | copy-start | bytes 746500 | tf_op jit(solution)/shard_map/while
  252.8 3.8 copy-start.3
  252.8 7.5 %copy-start.2 = (bf16[1,2,162,384]{3,2,1,0:T(8,128)(2,1)S(1)}, bf16[1,2,162,384]{3,2,1,0:T(8,128)(2,1)}, u32[]{:S(2)}) copy-start(bf16[1,2,162,384]{3,2,1,0:T(8,128)(2,1)} %get-tuple-element.300) | copy-start | bytes 746500 | tf_op jit(solution)/shard_map/while
  294.5 5.8 %copy-start.1 = (bf16[9,384,288]{2,1,0:T(8,128)(2,1)S(1)}, bf16[9,384,288]{2,1,0:T(8,128)(2,1)}, u32[]{:S(2)}) copy-start(bf16[9,384,288]{2,1,0:T(8,128)(2,1)} %copy-done) | copy-start | bytes 5971972 | tf_op jit(solution)/shard_map/while
  300.2 4.5 copy-start
  304.7 4.8 %copy-start.4 = (bf16[1,2,162,384]{3,2,1,0:T(8,128)(2,1)S(1)}, bf16[1,2,162,384]{3,2,1,0:T(8,128)(2,1)}, u32[]{:S(2)}) copy-start(bf16[1,2,162,384]{3,2,1,0:T(8,128)(2,1)} %get-tuple-element.297) | copy-start | bytes 746500 | tf_op jit(solution)/shard_map/while
  307.1 3.8 copy-start.3
  307.1 7.5 %copy-start.2 = (bf16[1,2,162,384]{3,2,1,0:T(8,128)(2,1)S(1)}, bf16[1,2,162,384]{3,2,1,0:T(8,128)(2,1)}, u32[]{:S(2)}) copy-start(bf16[1,2,162,384]{3,2,1,0:T(8,128)(2,1)} %get-tuple-element.300) | copy-start | bytes 746500 | tf_op jit(solution)/shard_map/while
  348.8 5.8 %copy-start.1 = (bf16[9,384,288]{2,1,0:T(8,128)(2,1)S(1)}, bf16[9,384,288]{2,1,0:T(8,128)(2,1)}, u32[]{:S(2)}) copy-start(bf16[9,384,288]{2,1,0:T(8,128)(2,1)} %copy-done) | copy-start | bytes 5971972 | tf_op jit(solution)/shard_map/while
  364.9 14.6 %copy-start.6 = (bf16[1,2,160,384]{3,2,1,0:T(8,128)(2,1)S(1)}, bf16[1,2,160,384]{3,2,1,0:T(8,128)(2,1)}, u32[]{:S(2)}) copy-start(bf16[1,2,160,384]{3,2,1,0:T(8,128)(2,1)} %param.11) | copy-start | bytes 737284
  364.9 14.7 %copy-start.10 = (bf16[1,2,160,384]{3,2,1,0:T(8,128)(2,1)S(1)}, bf16[1,2,160,384]{3,2,1,0:T(8,128)(2,1)}, u32[]{:S(2)}) copy-start(bf16[1,2,160,384]{3,2,1,0:T(8,128)(2,1)} %param.7) | copy-start | bytes 737284
  364.9 14.7 %copy-start.11 = (f32[1,2,160,384]{3,2,1,0:T(8,128)S(1)}, f32[1,2,160,384]{3,2,1,0:T(8,128)}, u32[]{:S(2)}) copy-start(f32[1,2,160,384]{3,2,1,0:T(8,128)} %get-tuple-element.215) | copy-start | bytes 1474564
  364.9 14.7 %copy-start.12 = (f32[384]{0:T(512)S(1)}, f32[384]{0:T(512)}, u32[]{:S(2)}) copy-start(f32[384]{0:T(512)} %param.9) | copy-start | bytes 4612
  364.9 13.9 %all-to-all-start.1 = ((f32[1,8,160,96]{3,2,0,1:T(8,128)}), f32[1,8,160,96]{3,2,0,1:T(8,128)S(1)}, u32[]{:S(2)}, u32[]{:S(2)}) async-start(f32[1,8,160,96]{3,2,0,1:T(8,128)} %bitcast.6), calls=%async_computation.1 | async-start | bytes 1310720 | tf_op jit(solution)/shard_map/all_to_all | solution.py:155
Sparse Core Ops, SparseCore 0:
  365.0 100.5 reduce-scatter.3
